TPU v7x, 32 devices: a whole 2x2x4 slice. The times are simulated.
32 devices in a mesh: grp: 2 (over x), cand: 8 (over z, y), seq: 2 (over core).
Axes of the slice: x: 2, y: 2, z: 4, core: 2. Of those that a mesh axis runs over, the one named last changes fastest.
Arguments:
- x_prefix: bfloat16 [8192, 2560], P(('grp', 'cand', 'seq')), parts along dimension 0, may hold values from -6 to 6
- b_prefix: bfloat16 [8192, 128], P(('grp', 'cand', 'seq')), parts along dimension 0, may hold values from -0.5 to 0.5
- code_prefix: int32 [8192, 40], P(('grp', 'cand', 'seq')), parts along dimension 0, may hold values from 0 to 500
- x_cand: bfloat16 [32, 512, 2560], P(('grp', 'cand'), None, 'seq'), parts along dimension 0, may hold values from -6 to 6
- b_cand: bfloat16 [32, 512, 128], P(('grp', 'cand')), parts along dimension 0, may hold values from -0.5 to 0.5
- c_cand: bfloat16 [32, 512, 128], P(('grp', 'cand')), parts along dimension 0, may hold values from -0.5 to 0.5
- code_cand: int32 [32, 512, 40], P(('grp', 'cand'), None, 'seq'), parts along dimension 0, may hold values from 0 to 500
- lengths: int32 [32], P(('grp', 'cand')), parts along dimension 0, may hold values from 1 to 2, as said below
- dy_cand: bfloat16 [32, 512, 2560], P(('grp', 'cand'), None, 'seq'), parts along dimension 0, may hold values from -1.5 to 1.5
Outputs:
- dx_prefix: bfloat16 [8192, 2560], P(('grp', 'cand', 'seq')), parts along dimension 0
- db_prefix: float32 [8192, 128], P(('grp', 'cand', 'seq')), parts along dimension 0
- dx_cand: bfloat16 [32, 512, 2560], P(('grp', 'cand'), None, 'seq'), parts along dimension 0
- db_cand: float32 [32, 512, 128], P(('grp', 'cand'), 'seq'), parts along dimension 0
- dc_cand: float32 [32, 512, 128], P(('grp', 'cand'), 'seq'), parts along dimension 0
There are 2 independent parts, one for each index of `grp`. A program takes and returns all parts, laid end to end along the dimension named above; each array names one. Nothing has to cross between parts.
Inputs may be any that keep to these rules, and one draw needn't show every extreme that they name: lengths count blocks of 256 tokens.
All inputs are finite; a program needn't handle non-finite values.
Results may differ from a plain program's by a relative error of at most 0.0015.
The roundings to bfloat16 on the way count: a program that leaves them out, or rounds other values in their place, can miss the bound.
Values may be sent and summed in bfloat16 or wider, within the bound.
No kernel may reach another device: no remote copies, remote signals or barrier semaphores. Data moves between devices by JAX's collectives and lax.ppermute only.
A program may use at most 256 MiB of HBM per device.

v0:
```python
import jax
import jax.numpy as jnp
from jax import lax
from jax.sharding import PartitionSpec as P

BLOCK = 256


def entering(shard, axis, combine, identity, reverse):
    length, mine = (lax.axis_size(axis), lax.axis_index(axis))
    everything = jax.tree.map(lambda part: lax.all_gather(part, axis), shard)
    start = jax.tree.map(
        lambda part, zero: jnp.broadcast_to(jnp.asarray(zero, part.dtype), part.shape),
        shard,
        identity,
    )

    def turn(k, before):
        at = length - 1 - k if reverse else k
        reached = at > mine if reverse else at < mine
        new = combine(before, jax.tree.map(lambda part: part[at], everything))
        return jax.tree.map(lambda a, b: jnp.where(reached, a, b), new, before)

    return lax.fori_loop(0, length, turn, start)


def broadcast(shard, axis, root):
    mine = lax.axis_index(axis) == root
    return lax.psum(jnp.where(mine, shard, jnp.zeros_like(shard)), axis)


def add_pair(earlier, later_part):
    return earlier + later_part


def link_states(earlier, later_part):
    return (
        earlier[0] * jnp.exp(later_part[1])[:, None, None] + later_part[0],
        earlier[1] + later_part[1],
    )


def candidate_terms(candidate, head_size):
    x_one, g_one, b_one, c_one, level_sum = candidate
    cand_len = x_one.shape[0]
    heads_total = level_sum.shape[1]
    position = jnp.arange(cand_len, dtype=jnp.int32)
    causal = position[:, None] >= position[None, :]
    scores = lax.dot_general(
        c_one, b_one, (((1,), (1,)), ((), ())), preferred_element_type=jnp.float32
    )

    def per_head(head_at, carry):
        weight_sum, grad_x = carry
        x_head = lax.dynamic_slice_in_dim(x_one, head_at * head_size, head_size, 1)
        g_head = lax.dynamic_slice_in_dim(g_one, head_at * head_size, head_size, 1)
        level_head = lax.dynamic_slice_in_dim(level_sum, head_at, 1, 1)[:, 0]
        decay_mat = jnp.where(
            causal, jnp.exp(level_head[:, None] - level_head[None, :]), jnp.zeros((), jnp.float32)
        )
        kernel = (scores * decay_mat).astype(jnp.bfloat16)
        dx_piece = lax.dot_general(
            kernel, g_head, (((0,), (0,)), ((), ())), preferred_element_type=jnp.float32
        )
        grad_x = lax.dynamic_update_slice_in_dim(
            grad_x, dx_piece.astype(jnp.bfloat16), head_at * head_size, 1
        )
        inner_prod = lax.dot_general(
            g_head, x_head, (((1,), (1,)), ((), ())), preferred_element_type=jnp.float32
        )
        return (weight_sum + inner_prod * decay_mat, grad_x)

    start = (jnp.zeros((cand_len, cand_len), jnp.float32), jnp.zeros_like(x_one))
    weight_sum, grad_x = lax.fori_loop(0, heads_total, per_head, start)
    db_part = jnp.dot(weight_sum.T, c_one.astype(jnp.float32), precision=lax.Precision.HIGHEST)
    dc_part = jnp.dot(weight_sum, b_one.astype(jnp.float32), precision=lax.Precision.HIGHEST)
    return (grad_x, db_part, dc_part)


def shards(x_prefix, b_prefix, code_prefix, x_cand, b_cand, c_cand, code_cand, lengths, dy_cand):
    pre_len, width = x_prefix.shape
    heads_total = code_prefix.shape[1]
    head_size = width // heads_total
    nstate = b_prefix.shape[1]
    cand_dev, cand_len, half_width = x_cand.shape
    half_heads = code_cand.shape[2]
    seq_at = lax.axis_index("seq")
    log_prefix = jnp.log1p(-code_prefix.astype(jnp.float32) * 1e-06)
    own_total = jnp.sum(log_prefix, axis=0)
    later_total = entering(own_total, ("cand", "seq"), add_pair, jnp.zeros_like(own_total), True)
    after_local = own_total[None, :] - jnp.cumsum(log_prefix, axis=0)
    weight = jnp.exp(after_local + later_total[None, :])
    weighted_b = (weight[:, :, None] * b_prefix[:, None, :].astype(jnp.float32)).astype(
        jnp.bfloat16
    )
    x_heads = x_prefix.reshape(pre_len, heads_total, head_size)
    state_full = jnp.einsum("jhp,jhn->hpn", x_heads, weighted_b, preferred_element_type=jnp.float32)
    own_state = state_full * jnp.exp(-later_total)[:, None, None]
    empty = (jnp.zeros_like(own_state), jnp.zeros_like(own_total))
    before = entering((own_state, own_total), ("cand", "seq"), link_states, empty, False)
    final_state = before[0] * jnp.exp(own_total)[:, None, None] + own_state
    root_last = lax.axis_size(("cand", "seq")) - 1
    whole_init = broadcast(final_state.astype(jnp.bfloat16), ("cand", "seq"), root_last)
    init_half = lax.dynamic_slice_in_dim(whole_init, seq_at * half_heads, half_heads, 0)
    position = jnp.arange(cand_len, dtype=jnp.int32)
    valid_rows = position[None, :] < lengths[:, None] * BLOCK
    g_cand = jnp.where(valid_rows[:, :, None], dy_cand, jnp.zeros_like(dy_cand))
    level_all = jnp.cumsum(jnp.log1p(-code_cand.astype(jnp.float32) * 1e-06), axis=1)

    def run_candidate(candidate):
        return candidate_terms(candidate, head_size)

    dx_cand, db_part, dc_part = lax.map(run_candidate, (x_cand, g_cand, b_cand, c_cand, level_all))
    amplitude = jnp.exp(level_all)
    g_heads = g_cand.reshape(cand_dev, cand_len, half_heads, head_size)
    decayed_g = (g_heads.astype(jnp.float32) * amplitude[:, :, :, None]).astype(jnp.bfloat16)
    dstate = jnp.einsum("cthp,ctn->hpn", decayed_g, c_cand, preferred_element_type=jnp.float32)
    dc_state = jnp.dot(
        decayed_g.reshape(cand_dev * cand_len, half_width),
        init_half.reshape(half_width, nstate),
        preferred_element_type=jnp.float32,
    )
    dc_total = dc_part + dc_state.reshape(cand_dev, cand_len, nstate)
    db_cand, dc_cand = (
        lax.psum_scatter(db_part, "seq", scatter_dimension=1, tiled=True),
        lax.psum_scatter(dc_total, "seq", scatter_dimension=1, tiled=True),
    )
    summed = lax.psum(dstate, "cand")
    grad_state = lax.all_gather(summed.astype(jnp.bfloat16), "seq", axis=0, tiled=True)
    dx_prefix = jnp.einsum(
        "jhn,hpn->jhp", weighted_b, grad_state, preferred_element_type=jnp.float32
    )
    dx_prefix = dx_prefix.astype(jnp.bfloat16).reshape(pre_len, width)
    projected = jnp.einsum("jhp,hpn->jhn", x_heads, grad_state, preferred_element_type=jnp.float32)
    db_prefix = jnp.sum(projected * weight[:, :, None], axis=1)
    return (dx_prefix, db_prefix, dx_cand, db_cand, dc_cand)


def solution(mesh):
    return jax.shard_map(
        shards,
        mesh=mesh,
        in_specs=(
            P(("grp", "cand", "seq"), None),
            P(("grp", "cand", "seq"), None),
            P(("grp", "cand", "seq"), None),
            P(("grp", "cand"), None, "seq"),
            P(("grp", "cand"), None, None),
            P(("grp", "cand"), None, None),
            P(("grp", "cand"), None, "seq"),
            P(("grp", "cand")),
            P(("grp", "cand"), None, "seq"),
        ),
        out_specs=(
            P(("grp", "cand", "seq"), None),
            P(("grp", "cand", "seq"), None),
            P(("grp", "cand"), None, "seq"),
            P(("grp", "cand"), "seq", None),
            P(("grp", "cand"), "seq", None),
        ),
        check_vma=False,
    )
```

profile of v0, /device:TPU:0, one launch (start us, length us, event | category | flops | bytes accessed | tf_op | source)
XLA Modules:
  0.0 392.8 jit_solution(4771028220192774179)
XLA Ops:
  11.1 34.9 %all-reduce = f32[640]{0:T(1024)S(1)} all-reduce(f32[640]{0:T(1024)S(1)} %dynamic-update-slice), channel_id=2, replica_groups=mesh['grp'=2,'cand'=8,'seq'=2] {'cand','seq'}, use_global_device_ids=true, to_apply=%add | all-reduce | flops 640 | bytes 5120
  47.9 1.6 copy.51
  49.6 2.1 fusion.40
  52.9 2.3 reduce-window.14
  55.7 4.6 %copy.43 = bf16[2,512,1280]{1,2,0:T(8,128)(2,1)} copy(bf16[2,512,1280]{2,1,0:T(8,128)(2,1)} %param.25) | data formatting | bytes 5242880 | tf_op args[8]
  60.4 5.0 %fusion.28 = (bf16[2,512,1280]{1,2,0:T(8,128)(2,1)}, bf16[2,512,1280]{1,2,0:T(8,128)(2,1)}) fusion(f32[2,512,20]{1,2,0:T(8,128)S(1)} %copy.46, bf16[2,512,1280]{1,2,0:T(8,128)(2,1)} %copy.43, pred[2,512]{1,0:T(4,128)(4,1)S(1)} %iota_compare_fusion.1), kind=kLoop, calls=%fused_computation.45 | loop fusion | flops 5242880 | bytes 7947264 | tf_op jit(solution)/shard_map/convert_element_type | solution.py:116
  65.4 92.7 %all-gather.4.cloned.1.call-done = f32[640,64,128]{2,1,0:T(8,128)} async-done(((f32[40,64,128]{2,1,0:T(8,128)}), f32[640,64,128]{2,1,0:T(8,128)}) %all-gather.4.cloned.1.call-update) | async-done | bytes 20971536 | tf_op jit(solution)/shard_map/all_gather | solution.py:11
  158.0 26.6 %while.63 = (s32[]{:T(128)}, f32[40,64,128]{2,1,0:T(8,128)S(1)}, s32[]{:T(128)}, f32[16,40]{1,0:T(8,128)S(1)}, f32[16,40,64,128]{3,2,1,0:T(8,128)}, /*index=5*/s32[]{:T(128)}, s32[]{:T(128)}) while((s32[]{:T(128)}, f32[40,64,128]{2,1,0:T(8,128)S(1)}, s32[]{:T(128)}, f32[16,40]{1,0:T(8,128)S(1)}, f32[16,40,64,128]{3,2,1,0:T(8,128)}, ...), condition=%wide.region_15.16_spmd.clone, body=%wide.region_14.15_spmd.clone.sunk | while | flops 1310724 | bytes 3932745 | solution.py:24
  158.1 1.7 fusion.82
  161.5 1.6 fusion.82
  163.1 1.6 fusion.82
  166.5 1.6 fusion.82
  168.1 1.6 fusion.82
  185.9 144.2 %while.61 = (s32[]{:T(128)}, bf16[2,512,1280]{2,1,0:T(8,128)(2,1)}, f32[2,512,128]{2,1,0:T(8,128)}, f32[2,512,128]{2,1,0:T(8,128)}, bf16[2,512,1280]{2,1,0:T(8,1...) while((s32[]{:T(128)}, bf16[2,512,1280]{2,1,0:T(8,128)(2,1)}, ...), condition=%wide.region_12.13_spmd, body=%wide.region_9.12_spmd.sunk | while | flops 942440448 | bytes 26593764 | solution.py:113
  190.0 2.5 dynamic-slice_bitcast_fusion.2
  192.6 59.2 %while.64 = (s32[]{:T(128)}, f32[512,512]{1,0:T(8,128)S(1)}, bf16[512,1280]{0,1:T(8,128)(2,1)S(1)}, bf16[512,1280]{1,0:T(8,128)(2,1)}, bf16[512,1280]{1,0:T(8,12...) while((s32[]{:T(128)}, f32[512,512]{1,0:T(8,128)S(1)}, ...), condition=%wide.region_11.11_spmd.clone, body=%wide.region_10.10_spmd.clone.sunk | while | flops 70025224 | bytes 3619496 | solution.py:74
  251.9 2.7 fusion.80
  262.2 2.5 dynamic-slice_bitcast_fusion.2
  264.8 59.2 %while.64 = (s32[]{:T(128)}, f32[512,512]{1,0:T(8,128)S(1)}, bf16[512,1280]{0,1:T(8,128)(2,1)S(1)}, bf16[512,1280]{1,0:T(8,128)(2,1)}, bf16[512,1280]{1,0:T(8,12...) while((s32[]{:T(128)}, f32[512,512]{1,0:T(8,128)S(1)}, ...), condition=%wide.region_11.11_spmd.clone, body=%wide.region_10.10_spmd.clone.sunk | while | flops 70025224 | bytes 3619496 | solution.py:74
  324.0 2.7 fusion.80
  331.3 3.6 convolution_add_fusion
  334.9 1.8 fusion.41
  336.8 42.5 %all-reduce.5 = bf16[20,64,128]{2,1,0:T(8,128)(2,1)S(1)} all-reduce(f32[20,64,128]{2,1,0:T(8,128)S(1)} %fusion.41), channel_id=1, replica_groups=mesh['grp'=2,'cand'=8,'seq'=2] {'cand'}, use_global_device_ids=true, to_apply=%region_2.3 | all-reduce | flops 163840 | bytes 983040 | tf_op jit(solution)/shard_map/psum | solution.py:128
  379.3 2.3 all_gather.15
  (269 shorter events, 162.2 us)
Async XLA Ops:
  8.0 150.0 %all-gather.4.cloned.1.call-start = ((), (), s32[]{:S(2)}) async-start(), calls=%async_computation.5 | async-start | bytes 22282240 | tf_op jit(solution)/shard_map/all_gather | solution.py:11
  47.8 1.8 copy-start.13
  47.8 1.6 copy-start.12
  49.5 2.2 copy-start.2
  49.6 2.1 copy-start.9
  51.7 0.9 copy-start.11
  51.8 278.5 %all-reduce.4.cloned.1.call-start = ((), (), s32[]{:S(2)}) async-start(), calls=%async_computation.3 | async-start | bytes 1310720 | tf_op jit(solution)/shard_map/psum | solution.py:29
  55.7 4.7 %copy-start.7 = (f32[2,512,20]{1,2,0:T(8,128)}, f32[2,512,20]{1,2,0:T(8,128)S(1)}, u32[]{:S(2)}) copy-start(f32[2,512,20]{1,2,0:T(8,128)S(1)} %copy.46) | copy-start | bytes 245764
  55.7 4.6 %copy-start.15 = (s32[2]{0:T(128)S(1)}, s32[2]{0:T(128)}, u32[]{:S(2)}) copy-start(s32[2]{0:T(128)} %param.24) | copy-start | bytes 28
  158.0 26.7 %copy-start.1 = (f32[40,64,128]{2,1,0:T(8,128)S(1)}, f32[40,64,128]{2,1,0:T(8,128)}, u32[]{:S(2)}) copy-start(f32[40,64,128]{2,1,0:T(8,128)} %fusion.40) | copy-start | bytes 3932164
  185.8 199.5 %reduce-scatter.3.cloned.1.call-start = ((), (), s32[]{:S(2)}) async-start(), calls=%async_computation.2 | async-start | bytes 786432 | tf_op jit(solution)/shard_map/reduce_scatter | solution.py:125
  251.9 2.7 copy-start.4
  256.1 0.8 copy-start.5
  324.0 2.7 copy-start.4
  328.2 0.8 copy-start.5
  330.1 1.2 copy-start.6
  330.2 55.2 %reduce-scatter.5.cloned.1.call-start = ((), (), s32[]{:S(2)}) async-start(), calls=%async_computation.4 | async-start | bytes 786432 | tf_op jit(solution)/shard_map/reduce_scatter | solution.py:126
  331.3 3.6 copy-start
  331.3 3.6 copy-start.8
  336.7 44.9 %copy-start.10 = (f32[256,128]{0,1:T(8,128)S(1)}, f32[256,128]{0,1:T(8,128)}, u32[]{:S(2)}) copy-start(f32[256,128]{0,1:T(8,128)} %copy-done.9) | copy-start | bytes 393220
  336.7 44.8 %copy-start.14 = (f32[256,40]{0,1:T(8,128)S(1)}, f32[256,40]{0,1:T(8,128)}, u32[]{:S(2)}) copy-start(f32[256,40]{0,1:T(8,128)} %copy-done.13) | copy-start | bytes 122884
  382.1 1.6 copy-start.3
Sparse Core Ops, SparseCore 0:
  51.9 106.1 all-gather.3
  186.0 91.2 all-reduce.3
Sparse Core Ops, SparseCore 1:
  330.2 7.9 reduce-scatter.2
  341.0 9.0 reduce-scatter.4
where the time goes:
time: 396 us; the launch traced here: 393 us
  matrix products  136 us (34%)
  waiting for transfers between devices  92.8 us (23%)
  blocking collectives  79.7 us (20%)
  other arithmetic  36.7 us (9%)
  local copies, waits for them, and re-layouts  28.1 us (7%)
  between operations  16.5 us (4%)
    all_gather x1, waiting for transfers between devices, entering(): everything = jax.tree.map(lambda part: lax.all_gather(part, axis), shard)  92.7 us
    dot_general x40, matrix products, per_head(): lax.dot_general(g_head, x_head, (((1,), (1,)), ((), ())), preferred_eleme...  63 us
    dot_general x40, matrix products, per_head(): lax.dot_general(kernel, g_head, (((0,), (0,)), ((), ())), preferred_eleme...  53.1 us
    psum x1, blocking collectives, shards(): summed = lax.psum(dstate, 'cand')  42.5 us
    unnamed x1, blocking collectives  34.9 us
    select_n x32, other arithmetic, turn(): return jax.tree.map(lambda a, b: jnp.where(reached, a, b), new, before)  26.3 us
    unnamed x35, local copies, waits for them, and re-layouts  10.9 us
  transfers between devices with their start and end apart: 4, of which 1 were waited for; matrix products, arithmetic and copies ran while one was open for 42% of the time, Pallas kernels for 0%

commit v1 on v0

--- a/solution.py
+++ b/solution.py
@@ -1,9 +1,17 @@
+import functools
 import jax
 import jax.numpy as jnp
 from jax import lax
 from jax.sharding import PartitionSpec as P
 
 BLOCK = 256
+
+
+def launch_layers_all_on(matrix, dev_axis):
+    return jnp.sum(lax.all_gather(matrix, dev_axis), axis=0)
+
+
+bind_waves_on_mesh = functools.partial(launch_layers_all_on, dev_axis="cand")
 
 
 def entering(shard, axis, combine, identity, reverse):
@@ -125,7 +133,7 @@
         lax.psum_scatter(db_part, "seq", scatter_dimension=1, tiled=True),
         lax.psum_scatter(dc_total, "seq", scatter_dimension=1, tiled=True),
     )
-    summed = lax.psum(dstate, "cand")
+    summed = bind_waves_on_mesh(dstate)
     grad_state = lax.all_gather(summed.astype(jnp.bfloat16), "seq", axis=0, tiled=True)
     dx_prefix = jnp.einsum(
         "jhn,hpn->jhp", weighted_b, grad_state, preferred_element_type=jnp.float32

time: 396 us -> 367 us (0.927)
  blocking collectives: 79.7 us -> 37.2 us
  waiting for transfers between devices: 92.8 us -> 108 us
    psum x1 -> x0, blocking collectives: 42.5 us -> none  [shards(): summed = lax.psum(dstate, 'cand')]
    all_gather x1, waiting for transfers between devices: 92.7 us -> 102 us  [entering(): everything = jax.tree.map(lambda part: lax.all_gather(part, axis), shard)]
    reduce_scatter x1, waiting for transfers between devices: 0.01 us -> 5.99 us  [shards(): lax.psum_scatter(dc_total, 'seq', scatter_dimension=1, tiled=True)]
    unnamed x35 -> x33, local copies, waits for them, and re-layouts: 10.9 us -> 10.9 us
  transfers between devices with their start and end apart: 4 -> 5, of which waited for: 1 -> 2; matrix products, arithmetic and copies ran while one was open for 42% -> 44% of each run, Pallas kernels for 0% -> 0%
where the time goes in v1:
time: 367 us; the launch traced here: 365 us
  matrix products  134 us (37%)
  waiting for transfers between devices  108 us (29%)
  other arithmetic  37.3 us (10%)
  blocking collectives  37.2 us (10%)
  local copies, waits for them, and re-layouts  28.1 us (8%)
  between operations  16.2 us (4%)
    all_gather x1, waiting for transfers between devices, entering(): everything = jax.tree.map(lambda part: lax.all_gather(part, axis), shard)  102 us
    dot_general x40, matrix products, per_head(): lax.dot_general(g_head, x_head, (((1,), (1,)), ((), ())), preferred_eleme...  63.1 us
    dot_general x40, matrix products, per_head(): lax.dot_general(kernel, g_head, (((0,), (0,)), ((), ())), preferred_eleme...  53.2 us
    unnamed x1, blocking collectives  34.9 us
    select_n x32, other arithmetic, turn(): return jax.tree.map(lambda a, b: jnp.where(reached, a, b), new, before)  26.3 us
    unnamed x33, local copies, waits for them, and re-layouts  10.9 us
  transfers between devices with their start and end apart: 5, of which 2 were waited for; matrix products, arithmetic and copies ran while one was open for 44% of the time, Pallas kernels for 0%

profile of v1, /device:TPU:0, one launch (start us, length us, event | category | flops | bytes accessed | tf_op | source)
XLA Modules:
  0.0 364.5 jit_solution(9388478137823456712)
XLA Ops:
  11.1 34.9 %all-reduce = f32[640]{0:T(1024)S(1)} all-reduce(f32[640]{0:T(1024)S(1)} %dynamic-update-slice), channel_id=3, replica_groups=mesh['grp'=2,'cand'=8,'seq'=2] {'cand','seq'}, use_global_device_ids=true, to_apply=%add | all-reduce | flops 640 | bytes 5120
  47.9 1.6 copy.51
  49.6 2.1 fusion.40
  52.9 2.3 reduce-window.14
  55.7 102.3 %all-gather.8.cloned.1.call-done = f32[640,64,128]{2,1,0:T(8,128)} async-done(((f32[40,64,128]{2,1,0:T(8,128)}), f32[640,64,128]{2,1,0:T(8,128)}) %all-gather.8.cloned.1.call-update) | async-done | bytes 20971536 | tf_op jit(solution)/shard_map/all_gather | solution.py:19
  158.0 26.6 %while.63 = (s32[]{:T(128)}, f32[40,64,128]{2,1,0:T(8,128)S(1)}, s32[]{:T(128)}, f32[16,40]{1,0:T(8,128)S(1)}, f32[16,40,64,128]{3,2,1,0:T(8,128)}, /*index=5*/s32[]{:T(128)}, s32[]{:T(128)}) while((s32[]{:T(128)}, f32[40,64,128]{2,1,0:T(8,128)S(1)}, s32[]{:T(128)}, f32[16,40]{1,0:T(8,128)S(1)}, f32[16,40,64,128]{3,2,1,0:T(8,128)}, ...), condition=%wide.region_15.16_spmd.clone, body=%wide.region_14.15_spmd.clone.sunk | while | flops 1310724 | bytes 3932745 | solution.py:32
  158.1 1.7 fusion.82
  161.5 1.6 fusion.82
  163.1 1.6 fusion.82
  186.0 3.0 copy.43
  189.0 2.3 fusion.28
  192.9 1.7 fusion.41
  194.7 142.7 %while.61 = (s32[]{:T(128)}, bf16[2,512,1280]{2,1,0:T(8,128)(2,1)}, f32[2,512,128]{2,1,0:T(8,128)}, f32[2,512,128]{2,1,0:T(8,128)}, bf16[2,512,1280]{2,1,0:T(8,1...) while((s32[]{:T(128)}, bf16[2,512,1280]{2,1,0:T(8,128)(2,1)}, ...), condition=%wide.region_12.13_spmd, body=%wide.region_9.12_spmd.sunk | while | flops 942440448 | bytes 27642368 | solution.py:121
  198.8 2.5 dynamic-slice_bitcast_fusion.2
  201.5 59.4 %while.64 = (s32[]{:T(128)}, f32[512,512]{1,0:T(8,128)S(1)}, bf16[512,1280]{0,1:T(8,128)(2,1)S(1)}, bf16[512,1280]{1,0:T(8,128)(2,1)}, bf16[512,1280]{1,0:T(8,12...) while((s32[]{:T(128)}, f32[512,512]{1,0:T(8,128)S(1)}, ...), condition=%wide.region_11.11_spmd.clone, body=%wide.region_10.10_spmd.clone.sunk | while | flops 70025224 | bytes 3619496 | solution.py:82
  234.2 1.6 fusion.86
  260.9 2.7 fusion.80
  270.3 2.5 dynamic-slice_bitcast_fusion.2
  272.9 59.2 %while.64 = (s32[]{:T(128)}, f32[512,512]{1,0:T(8,128)S(1)}, bf16[512,1280]{0,1:T(8,128)(2,1)S(1)}, bf16[512,1280]{1,0:T(8,128)(2,1)}, bf16[512,1280]{1,0:T(8,12...) while((s32[]{:T(128)}, f32[512,512]{1,0:T(8,128)S(1)}, ...), condition=%wide.region_11.11_spmd.clone, body=%wide.region_10.10_spmd.clone.sunk | while | flops 70025224 | bytes 3619496 | solution.py:82
  332.1 2.7 fusion.80
  338.5 3.4 convolution_add_fusion
  342.0 3.3 reduce_sum.27
  345.3 2.3 all_gather.23
  351.4 6.0 %reduce-scatter.5.cloned.1.call-done = f32[2,256,128]{2,1,0:T(8,128)} async-done(((f32[2,512,128]{2,1,0:T(8,128)}), f32[2,256,128]{2,1,0:T(8,128)}) %reduce-scatter.5.cloned.1.call-update) | async-done | bytes 262160 | tf_op jit(solution)/shard_map/reduce_scatter | solution.py:134
  (274 shorter events, 163.9 us)
Async XLA Ops:
  8.0 150.0 %all-gather.8.cloned.1.call-start = ((), (), s32[]{:S(2)}) async-start(), calls=%async_computation.6 | async-start | bytes 22282240 | tf_op jit(solution)/shard_map/all_gather | solution.py:19
  47.8 1.8 copy-start.13
  47.8 1.6 copy-start.12
  49.5 2.2 copy-start.4
  49.6 2.1 copy-start.9
  51.7 0.9 copy-start.11
  51.7 3.9 %copy-start.15 = (s32[2]{0:T(128)S(1)}, s32[2]{0:T(128)}, u32[]{:S(2)}) copy-start(s32[2]{0:T(128)} %param.24) | copy-start | bytes 28
  51.8 285.7 %all-reduce.3.cloned.1.call-start = ((), (), s32[]{:S(2)}) async-start(), calls=%async_computation.3 | async-start | bytes 1310720 | tf_op jit(solution)/shard_map/psum | solution.py:37
  158.0 26.7 %copy-start.3 = (f32[40,64,128]{2,1,0:T(8,128)S(1)}, f32[40,64,128]{2,1,0:T(8,128)}, u32[]{:S(2)}) copy-start(f32[40,64,128]{2,1,0:T(8,128)} %fusion.40) | copy-start | bytes 3932164
  185.9 156.1 %all-gather.6.cloned.1.call-start = ((), (), s32[]{:S(2)}) async-start(), calls=%async_computation.5 | async-start | bytes 5898240 | tf_op jit(solution)/shard_map/all_gather | solution.py:11
  189.0 3.9 %copy-start.1 = (bf16[2,512,128]{2,1,0:T(8,128)(2,1)S(1)}, bf16[2,512,128]{2,1,0:T(8,128)(2,1)}, u32[]{:S(2)}) copy-start(bf16[2,512,128]{2,1,0:T(8,128)(2,1)} %param.22) | copy-start | bytes 786436
  191.3 1.6 copy-start
  194.6 156.8 %reduce-scatter.3.cloned.1.call-start = ((), (), s32[]{:S(2)}) async-start(), calls=%async_computation.2 | async-start | bytes 786432 | tf_op jit(solution)/shard_map/reduce_scatter | solution.py:133
  260.9 2.7 copy-start.2
  260.9 2.7 copy-start.6
  264.2 0.8 copy-start.7
  332.1 2.7 copy-start.2
  332.1 2.7 copy-start.6
  335.5 0.8 copy-start.7
  337.4 1.2 copy-start.8
  337.4 20.0 %reduce-scatter.5.cloned.1.call-start = ((), (), s32[]{:S(2)}) async-start(), calls=%async_computation.4 | async-start | bytes 786432 | tf_op jit(solution)/shard_map/reduce_scatter | solution.py:134
  342.0 5.6 %copy-start.10 = (f32[256,128]{0,1:T(8,128)S(1)}, f32[256,128]{0,1:T(8,128)}, u32[]{:S(2)}) copy-start(f32[256,128]{0,1:T(8,128)} %copy-done.9) | copy-start | bytes 393220
  342.0 5.6 %copy-start.14 = (f32[256,40]{0,1:T(8,128)S(1)}, f32[256,40]{0,1:T(8,128)}, u32[]{:S(2)}) copy-start(f32[256,40]{0,1:T(8,128)} %copy-done.13) | copy-start | bytes 122884
  348.1 1.6 copy-start.5
Sparse Core Ops, SparseCore 0:
  51.9 106.1 all-gather.7
  186.0 131.5 all-reduce.2
  337.5 7.9 reduce-scatter.2
  348.2 9.1 reduce-scatter.4
Sparse Core Ops, SparseCore 1:
  194.7 88.0 all-gather.5
